TPU v7x, 256 devices: a whole 4x4x8 slice. The times are simulated.
256 devices in a mesh: tm: 8 (over y_lo, x), stn: 32 (over y_hi, z, core).
Axes of the slice: x: 4, y: 4 (y_hi: 2, y_lo: 2; y = y_hi * 2 + y_lo), z: 8, core: 2. Of those that a mesh axis runs over, the one named last changes fastest.
Arguments:
- voltages: bfloat16 [1024, 524288], P('stn', 'tm'), may hold values from -6 to 6
- gains: float32 [2, 1024, 256], P(None, 'stn'), may hold values from -4 to 4
Outputs:
- visibility: float32 [256, 2, 1024, 1024], P(('tm', 'stn'))
All inputs are finite; a program needn't handle non-finite values.
Results may differ from a plain program's by a relative error of at most 0.0038.
Values may be sent and summed in bfloat16 or wider, within the bound.
No kernel may reach another device: no remote copies, remote signals or barrier semaphores. Data moves between devices by JAX's collectives and lax.ppermute only.
A program may use at most 128 MiB of HBM per device.

v0:
```python
import numpy as np
import jax
import jax.numpy as jnp
from jax import lax
from jax.sharding import PartitionSpec as P

CHANNELS = 4096
BAND_LOW = 1024
TAPS = 8


def passed_along(x, axis, by):
    devices = lax.axis_size(axis)
    pairs = [(i, i + by) for i in range(devices) if 0 <= i + by < devices]
    return lax.ppermute(x, axis, pairs)


def window_table(chans):
    frame_len = 2 * chans
    total_len = TAPS * frame_len
    positions = np.arange(total_len, dtype=np.float64)
    centred = (positions - (total_len - 1) / 2.0) / frame_len
    taper = np.sin(np.pi * (positions + 0.5) / total_len)
    shaped = np.sinc(centred) * taper * taper
    shaped = shaped / np.sqrt(np.sum(shaped * shaped))
    return shaped.reshape(TAPS, frame_len).astype(np.float32)


def split(x):
    hi = lax.reduce_precision(x, exponent_bits=8, mantissa_bits=7)
    lo = x - hi
    return (hi.astype(jnp.bfloat16), lo.astype(jnp.bfloat16))


def band_tables(frame_len, band):
    half = band // 2
    n_b = 32
    n_a = frame_len // 2 // n_b
    q = jnp.arange(2, dtype=jnp.int32)[:, None, None]
    k = jnp.arange(band, dtype=jnp.int32)[None, None, :]
    chan = 2 * (k % half) + q
    imag_col = k >= half
    a = jnp.arange(n_a, dtype=jnp.int32)[None, :, None]
    b = jnp.arange(n_b, dtype=jnp.int32)[None, :, None]
    p_steps = n_a * 2
    tp = 2.0 * jnp.pi / p_steps * (a * chan % p_steps).astype(jnp.float32)
    tq = 2.0 * jnp.pi / frame_len * (b * (BAND_LOW + chan) % frame_len).astype(jnp.float32)
    pr, pi = (jnp.cos(tp), -jnp.sin(tp))
    qr, qi = (jnp.cos(tq), -jnp.sin(tq))
    b1 = jnp.where(imag_col, qi, qr)
    b2 = jnp.where(imag_col, qr, -qi)
    t = pr[:, :, None, :] * b1[:, None, :, :] + pi[:, :, None, :] * b2[:, None, :, :]
    return split(t.reshape(2, n_a * n_b, band))


def on_device(voltages, gains):
    in_dev, length = voltages.shape
    band = gains.shape[2]
    half_band = band // 2
    frame_len = 2 * CHANNELS
    half_len = frame_len // 2
    frames = length // frame_len
    n_time = lax.axis_size("tm")
    n_station = lax.axis_size("stn")
    all_inputs = in_dev * n_station
    history = TAPS - 1
    slots = frames + history
    window = jnp.asarray(window_table(CHANNELS))
    t_hi, t_lo = band_tables(frame_len, band)
    framed = voltages.reshape(in_dev, frames, frame_len)
    pad = jnp.zeros((in_dev, history, frame_len), voltages.dtype)
    padded = jnp.concatenate([pad, framed, pad], axis=1).astype(jnp.float32)
    windowed = window[0] * padded[:, 0:slots, :]
    for tap_index in range(1, TAPS):
        windowed = windowed + window[tap_index] * padded[:, tap_index : tap_index + slots, :]
    first, second = (windowed[..., :half_len], windowed[..., half_len:])
    folded = jnp.stack([first + second, first - second])
    l_hi, l_lo = split(folded)
    lhs = jnp.stack([l_hi, l_lo], axis=1)
    f32 = jnp.float32
    part_hi = jnp.einsum("qhism,qmk->qhisk", lhs, t_hi, preferred_element_type=f32)
    part_lo = jnp.einsum("qism,qmk->qisk", l_hi, t_lo, preferred_element_type=f32)
    raw = part_hi[:, 0] + part_hi[:, 1] + part_lo
    own = raw[:, :, :frames, :]
    given = passed_along(raw[:, :, frames:, :], "tm", 1)
    own = own.at[:, :, :history, :].add(given)
    own = own.reshape(2, in_dev, frames, 2, half_band)
    raw_re = jnp.transpose(own[:, :, :, 0, :], (3, 0, 1, 2))
    raw_im = jnp.transpose(own[:, :, :, 1, :], (3, 0, 1, 2))
    g = jnp.transpose(gains.reshape(2, in_dev, half_band, 2), (0, 2, 3, 1))[..., None]
    gain_re, gain_im = (g[0], g[1])
    spec_re = gain_re * raw_re - gain_im * raw_im
    spec_im = gain_re * raw_im + gain_im * raw_re
    spectra = jnp.stack([spec_re, spec_im], axis=3).astype(jnp.bfloat16)
    row = in_dev * 2 * frames
    spectra = spectra.reshape(n_time, n_station, row)
    spectra = lax.all_to_all(spectra, "tm", split_axis=0, concat_axis=0, tiled=True)
    spectra = lax.all_to_all(spectra, "stn", split_axis=1, concat_axis=1, tiled=True)
    spectra = spectra.reshape(n_time, n_station, in_dev, 2, frames)
    spectra = jnp.transpose(spectra, (1, 2, 3, 0, 4)).reshape(all_inputs, 2, n_time * frames)
    stacked = spectra.reshape(all_inputs, 2 * n_time * frames)
    flipped = jnp.concatenate([spectra[:, 1], -spectra[:, 0]], axis=-1)
    both = jnp.concatenate([stacked, flipped], axis=0)
    vis = jnp.einsum("ik,jk->ij", both, stacked, preferred_element_type=f32)
    vis = vis * (1.0 / float(n_time * frames))
    return vis.reshape(1, 2, all_inputs, all_inputs)


def solution(mesh):
    in_specs = (P("stn", "tm"), P(None, "stn", None))
    out_specs = P(("tm", "stn"), None, None, None)
    return jax.shard_map(
        on_device, mesh=mesh, in_specs=in_specs, out_specs=out_specs, check_vma=False
    )
```

profile of v0, /device:TPU:1, one launch (start us, length us, event | category | flops | bytes accessed | tf_op | source)
XLA Modules:
  0.0 175.2 jit_solution(2518422193169905856)
XLA Ops:
  0.0 1.0 fusion.43
  1.1 0.3 negate_select_fusion.4
  1.4 1.2 multiply_add_fusion
  2.6 0.0 copy-start.1
  2.6 5.4 %reduce-precision_convert_fusion.1 = (bf16[2,4096,256]{2,1,0:T(8,128)(2,1)}, bf16[2,4096,256]{2,1,0:T(8,128)(2,1)}) fusion(f32[2,128,32,256]{3,2,1,0:T(8,128)S(1)} %multiply_add_fusion), kind=kLoop, calls=%fused_computation.26 | loop fusion | flops 8388608 | bytes 16777216 | tf_op jit(solution)/shard_map/convert_element_type | solution.py:32
  8.0 0.0 copy-done.1
  8.0 0.3 copy.60
  8.3 0.4 broadcast_in_dim.15
  8.7 0.0 copy-start.3
  8.7 0.0 copy-start.4
  8.7 0.0 copy-start.5
  8.7 0.0 copy-start.6
  8.7 0.0 copy-start.7
  8.7 0.0 copy-start.8
  8.7 0.0 copy-start.9
  8.8 0.0 copy-start.10
  8.8 8.0 %maximum_convert_fusion = f32[32,22,8192]{2,0,1:T(8,128)} fusion(bf16[32,7,8192]{2,0,1:T(8,128)(2,1)S(1)} %broadcast_in_dim.15, bf16[32,8,8192]{2,0,1:T(8,128)(2,1)S(1)} %bitcast.87), kind=kLoop, calls=%fused_computation.27 | loop fusion | flops 17301504 | bytes 30932992 | tf_op jit(solution)/shard_map/convert_element_type | solution.py:72
  16.7 0.0 copy-done.3
  16.7 0.0 copy-done.4
  16.7 0.0 copy-done.5
  16.7 0.0 copy-done.6
  16.8 0.0 copy-done.7
  16.8 50.0 %fusion.1 = f32[32,15,8192]{2,0,1:T(8,128)} fusion(f32[32,22,8192]{2,0,1:T(8,128)} %maximum_convert_fusion, f32[8192]{0:T(1024)S(1)} %copy-done.3, f32[8192]{0:T(1024)S(1)} %copy-done.4, f32[8192]{0:T(1024)S(1)} %copy-done.5, f32[8192]{0:T(1024)S(1)} %copy-done.6, f32[8192]{0:T(1024)S(1)} %copy-done.7, f32[8192]{0:T(1024)S(1)} %copy-done.8, ...), kind=kLoop, calls=%fused_computation.4 | loop fusion | flops 58982400 | bytes 141819904 | tf_op jit(solution)/shard_map/add | solution.py:75
  66.8 13.2 %fusion.19 = (f32[1,1,32,15,4096]{4,2,3,1,0:T(8,128)S(1)}, f32[1,32,15,4096]{3,1,2,0:T(8,128)}, f32[1,32,15,4096]{3,1,2,0:T(8,128)}, f32[1,1,32,15,4096]{4,2,3,1,0:T(8,128)}) fusion(f32[32,15,8192]{2,0,1:T(8,128)} %fusion.1), kind=kLoop, calls=%fused_computation.38 | loop fusion | flops 3932160 | bytes 47185920 | tf_op jit(solution)/shard_map/stack | solution.py:77
  80.0 5.3 %reduce-precision_convert_fusion = (bf16[2,1,32,15,4096]{4,2,3,1,0:T(8,128)(2,1)S(1)}, bf16[2,1,32,15,4096]{4,2,3,1,0:T(8,128)(2,1)S(1)}) fusion(f32[1,1,32,15,4096]{4,2,3,1,0:T(8,128)} %get-tuple-element.22, f32[1,1,32,15,4096]{4,2,3,1,0:T(8,128)S(1)} %get-tuple-element.19), kind=kLoop, calls=%fused_computation.1 | loop fusion | flops 19660800 | bytes 31457280 | tf_op jit(solution)/shard_map/convert_element_type | solution.py:32
  85.4 0.0 copy-start
  85.4 7.1 %fusion.8 = f32[2,2,32,15,256]{4,2,3,1,0:T(8,128)} fusion(bf16[2,1,32,15,4096]{4,2,3,1,0:T(8,128)(2,1)S(1)} %get-tuple-element.18, bf16[2,1,32,15,4096]{4,2,3,1,0:T(8,128)(2,1)S(1)} %get-tuple-element.17, bf16[2,4096,256]{2,1,0:T(8,128)(2,1)} %get-tuple-element.23), kind=kOutput, calls=%fused_computation.19 | convolution fusion | flops 4034396160 | bytes 21889024 | tf_op jit(solution)/shard_map/qhism,qmk->qhisk/dot_general | solution.py:81
  92.5 7.3 %fusion.22 = f32[2,32,15,256]{3,1,2,0:T(8,128)S(1)} fusion(bf16[2,4096,256]{2,1,0:T(8,128)(2,1)} %get-tuple-element.24, f32[1,32,15,4096]{3,1,2,0:T(8,128)S(1)} %copy-done, f32[1,32,15,4096]{3,1,2,0:T(8,128)} %get-tuple-element.21, f32[2,2,32,15,256]{4,2,3,1,0:T(8,128)} %fusion.8), kind=kOutput, calls=%fused_computation.41 | convolution fusion | flops 2025553920 | bytes 22872064 | tf_op jit(solution)/shard_map/qism,qmk->qisk/dot_general | solution.py:82
  99.8 4.2 %collective-permute-start = (f32[2,32,7,256]{3,1,2,0:T(8,128)S(1)}, f32[2,32,7,256]{3,1,2,0:T(8,128)S(1)}, u32[]{:S(2)}, u32[]{:S(2)}) collective-permute-start(f32[2,32,7,256]{3,1,2,0:T(8,128)S(1)} %slice.160), channel_id=1, source_target_pairs={{0,32},{32,64},{64,96},{96,128},{128,160},{160,192},{192,224},{1,3... | collective-permute-start | bytes 1376264 | tf_op jit(solution)/shard_map/ppermute | solution.py:15
  104.0 0.0 copy-done.2
  104.1 0.1 copy.25
  104.2 0.1 copy.29
  104.3 0.1 copy.26
  104.4 8.6 %collective-permute-done = f32[2,32,7,256]{3,1,2,0:T(8,128)S(1)} collective-permute-done((f32[2,32,7,256]{3,1,2,0:T(8,128)S(1)}, f32[2,32,7,256]{3,1,2,0:T(8,128)S(1)}, u32[]{:S(2)}, u32[]{:S(2)}) %collective-permute-start) | collective-permute-done | bytes 458784 | tf_op jit(solution)/shard_map/ppermute | solution.py:15
  112.9 0.1 fusion.33
  113.0 0.3 reshape.268
  113.3 0.6 fusion.57
  113.8 0.3 fusion.40
  114.2 6.7 %copy.31 = bf16[128,2,32,2,8]{4,3,2,1,0:T(2,128)(2,1)} copy(bf16[128,2,32,2,8]{0,4,3,2,1:T(8,128)(2,1)S(1)} %pad_maximum_fusion.1) | data formatting | bytes 524288 | tf_op jit(solution)/shard_map/stack | solution.py:94
  121.0 7.0 %convert_element_type.68 = bf16[8,32,512]{2,1,0:T(8,128)(2,1)S(1)} reshape(bf16[128,2,32,2,8]{4,3,2,1,0:T(2,128)(2,1)} %copy.31) | data formatting | bytes 524288 | tf_op jit(solution)/shard_map/convert_element_type | solution.py:94
  128.0 11.9 %all_to_all.10 = bf16[8,32,512]{2,1,0:T(8,128)(2,1)S(1)} all-to-all(bf16[8,32,512]{2,1,0:T(8,128)(2,1)S(1)} %convert_element_type.68), channel_id=1, replica_groups=mesh['tm'=8,'stn'=32] {'tm'}, dimensions={0} | all-to-all | bytes 524288 | tf_op jit(solution)/shard_map/all_to_all | solution.py:97
  140.0 0.1 copy.32
  140.1 26.8 %all_to_all.11 = bf16[8,32,512]{2,0,1:T(8,128)(2,1)S(1)} all-to-all(bf16[8,32,512]{2,0,1:T(8,128)(2,1)S(1)} %copy.32), channel_id=1, replica_groups=mesh['tm'=8,'stn'=32] {'stn'}, dimensions={1} | all-to-all | bytes 524288 | tf_op jit(solution)/shard_map/all_to_all | solution.py:98
  166.9 0.5 copy.33
  167.4 0.9 copy.34
  168.3 1.1 reshape_reshape.3
  169.4 1.1 reshape.270
  170.5 4.7 %convolution_multiply_fusion = f32[2048,1024]{1,0:T(8,128)} fusion(bf16[1024,128]{0,1:T(8,128)(2,1)S(1)} %reshape_reshape.3, bf16[1024,64]{0,1:T(8,128)(2,1)S(1)} %get-tuple-element.30, bf16[1024,64]{0,1:T(8,128)(2,1)S(1)} %get-tuple-element.29), kind=kOutput, calls=%fused_computation.33 | convolution fusion | flops 540540928 | bytes 8912896 | tf_op jit(solution)/shard_map/ik,jk->ij/dot_general | solution.py:104
  (13 shorter events, 0.2 us)
Async XLA Ops:
  2.6 5.4 %copy-start.1 = (bf16[32,65536]{1,0:T(8,128)(2,1)S(1)}, bf16[32,65536]{1,0:T(8,128)(2,1)}, u32[]{:S(2)}) copy-start(bf16[32,65536]{1,0:T(8,128)(2,1)} %param.5) | copy-start | bytes 12582916
  8.7 8.1 %copy-start.3 = (f32[8192]{0:T(1024)S(1)}, f32[8192]{0:T(1024)}, u32[]{:S(2)}) copy-start(f32[8192]{0:T(1024)} %constant.101) | copy-start | bytes 98308
  8.7 8.1 %copy-start.4 = (f32[8192]{0:T(1024)S(1)}, f32[8192]{0:T(1024)}, u32[]{:S(2)}) copy-start(f32[8192]{0:T(1024)} %constant.99) | copy-start | bytes 98308
  8.7 8.0 %copy-start.5 = (f32[8192]{0:T(1024)S(1)}, f32[8192]{0:T(1024)}, u32[]{:S(2)}) copy-start(f32[8192]{0:T(1024)} %constant.97) | copy-start | bytes 98308
  8.7 8.0 %copy-start.6 = (f32[8192]{0:T(1024)S(1)}, f32[8192]{0:T(1024)}, u32[]{:S(2)}) copy-start(f32[8192]{0:T(1024)} %constant.95) | copy-start | bytes 98308
  8.7 8.0 %copy-start.7 = (f32[8192]{0:T(1024)S(1)}, f32[8192]{0:T(1024)}, u32[]{:S(2)}) copy-start(f32[8192]{0:T(1024)} %constant.93) | copy-start | bytes 98308
  8.7 8.0 %copy-start.8 = (f32[8192]{0:T(1024)S(1)}, f32[8192]{0:T(1024)}, u32[]{:S(2)}) copy-start(f32[8192]{0:T(1024)} %constant.91) | copy-start | bytes 98308
  8.7 8.0 %copy-start.9 = (f32[8192]{0:T(1024)S(1)}, f32[8192]{0:T(1024)}, u32[]{:S(2)}) copy-start(f32[8192]{0:T(1024)} %constant.89) | copy-start | bytes 98308
  8.8 8.0 %copy-start.10 = (f32[8192]{0:T(1024)S(1)}, f32[8192]{0:T(1024)}, u32[]{:S(2)}) copy-start(f32[8192]{0:T(1024)} %constant.87) | copy-start | bytes 98308
  85.4 7.1 %copy-start = (f32[1,32,15,4096]{3,1,2,0:T(8,128)S(1)}, f32[1,32,15,4096]{3,1,2,0:T(8,128)}, u32[]{:S(2)}) copy-start(f32[1,32,15,4096]{3,1,2,0:T(8,128)} %get-tuple-element.20) | copy-start | bytes 23592964
  92.5 11.6 %copy-start.2 = (f32[2,32,256]{2,1,0:T(8,128)S(1)}, f32[2,32,256]{2,1,0:T(8,128)}, u32[]{:S(2)}) copy-start(f32[2,32,256]{2,1,0:T(8,128)} %param.6) | copy-start | bytes 196612
  99.8 13.1 %collective-permute-start = (f32[2,32,7,256]{3,1,2,0:T(8,128)S(1)}, f32[2,32,7,256]{3,1,2,0:T(8,128)S(1)}, u32[]{:S(2)}, u32[]{:S(2)}) collective-permute-start(f32[2,32,7,256]{3,1,2,0:T(8,128)S(1)} %slice.160), channel_id=1, source_target_pairs={{0,32},{32,64},{64,96},{96,128},{128,160},{160,192},{192,224},{1,3... | collective-permute-start | bytes 1376264 | tf_op jit(solution)/shard_map/ppermute | solution.py:15
where the time goes:
time: 175 us
  other arithmetic  84.9 us (49%)
  blocking collectives  38.7 us (22%)
  local copies, waits for them, and re-layouts  19.4 us (11%)
  matrix products  19 us (11%)
  waiting for transfers between devices  8.58 us (5%)
  starting transfers between devices  4.18 us (2%)
    add x1, other arithmetic, on_device(): windowed + window[tap_index] * padded[:, tap_index:tap_index + slots, :]  50 us
    all_to_all x1, blocking collectives, on_device(): lax.all_to_all(spectra, 'stn', split_axis=1, concat_axis=1, tiled=True)  26.8 us
    another operation x1, other arithmetic, on_device(): folded = jnp.stack([first + second, first - second])  13.2 us
    all_to_all x1, blocking collectives, on_device(): lax.all_to_all(spectra, 'tm', split_axis=0, concat_axis=0, tiled=True)  11.9 us
    convert_element_type x2, other arithmetic, split(): return (hi.astype(jnp.bfloat16), lo.astype(jnp.bfloat16))  10.7 us
    ppermute x1, waiting for transfers between devices, passed_along(): return lax.ppermute(x, axis, pairs)  8.58 us
    convert_element_type x1, other arithmetic, on_device(): padded = jnp.concatenate([pad, framed, pad], axis=1).astype(jnp.float32)  7.96 us
    dot_general x1, matrix products, on_device(): jnp.einsum('qism,qmk->qisk', l_hi, t_lo, preferred_element_type=f32)  7.27 us
  transfers between devices with their start and end apart: 1, of which 1 were waited for; matrix products, arithmetic and copies ran while one was open for 0% of the time, Pallas kernels for 0%

commit v1 on v0

--- a/solution.py
+++ b/solution.py
@@ -95,7 +95,10 @@
     row = in_dev * 2 * frames
     spectra = spectra.reshape(n_time, n_station, row)
     spectra = lax.all_to_all(spectra, "tm", split_axis=0, concat_axis=0, tiled=True)
-    spectra = lax.all_to_all(spectra, "stn", split_axis=1, concat_axis=1, tiled=True)
+    spectra = jnp.concatenate(
+        lax.all_to_all(jnp.stack(jnp.split(spectra, lax.axis_size("stn"), axis=1)), "stn", 0, 0),
+        axis=1,
+    )
     spectra = spectra.reshape(n_time, n_station, in_dev, 2, frames)
     spectra = jnp.transpose(spectra, (1, 2, 3, 0, 4)).reshape(all_inputs, 2, n_time * frames)
     stacked = spectra.reshape(all_inputs, 2 * n_time * frames)

time: 175 us -> 176 us (level)
  no operation moved by 1% of the time
where the time goes in v1:
time: 176 us
  other arithmetic  85 us (48%)
  blocking collectives  38.7 us (22%)
  local copies, waits for them, and re-layouts  20 us (11%)
  matrix products  19 us (11%)
  waiting for transfers between devices  8.59 us (5%)
  starting transfers between devices  4.19 us (2%)
    add x1, other arithmetic, on_device(): windowed + window[tap_index] * padded[:, tap_index:tap_index + slots, :]  50 us
    all_to_all x1, blocking collectives, on_device(): lax.all_to_all(jnp.stack(jnp.split(spectra, lax.axis_size('stn'), axis=1)...  26.8 us
    another operation x1, other arithmetic, on_device(): folded = jnp.stack([first + second, first - second])  13.2 us
    all_to_all x1, blocking collectives, on_device(): lax.all_to_all(spectra, 'tm', split_axis=0, concat_axis=0, tiled=True)  11.9 us
    convert_element_type x2, other arithmetic, split(): return (hi.astype(jnp.bfloat16), lo.astype(jnp.bfloat16))  10.7 us
    ppermute x1, waiting for transfers between devices, passed_along(): return lax.ppermute(x, axis, pairs)  8.59 us
    convert_element_type x1, other arithmetic, on_device(): padded = jnp.concatenate([pad, framed, pad], axis=1).astype(jnp.float32)  8.01 us
    dot_general x1, matrix products, on_device(): jnp.einsum('qism,qmk->qisk', l_hi, t_lo, preferred_element_type=f32)  7.27 us
  transfers between devices with their start and end apart: 1, of which 1 were waited for; matrix products, arithmetic and copies ran while one was open for 0% of the time, Pallas kernels for 0%

profile of v1, /device:TPU:1, one launch (start us, length us, event | category | flops | bytes accessed | tf_op | source)
XLA Modules:
  0.0 176.1 jit_solution(2995877657555908953)
XLA Ops:
  0.0 1.0 fusion.47
  1.1 0.3 negate_select_fusion.4
  1.4 1.2 multiply_add_fusion
  2.6 0.0 copy-start.1
  2.6 5.4 %reduce-precision_convert_fusion.1 = (bf16[2,4096,256]{2,1,0:T(8,128)(2,1)}, bf16[2,4096,256]{2,1,0:T(8,128)(2,1)}) fusion(f32[2,128,32,256]{3,2,1,0:T(8,128)S(1)} %multiply_add_fusion), kind=kLoop, calls=%fused_computation.26 | loop fusion | flops 8388608 | bytes 16777216 | tf_op jit(solution)/shard_map/convert_element_type | solution.py:32
  8.0 0.0 copy-done.1
  8.0 0.3 copy.904
  8.3 0.4 broadcast_in_dim.15
  8.7 0.0 copy-start.3
  8.7 0.0 copy-start.4
  8.7 0.0 copy-start.5
  8.7 0.0 copy-start.6
  8.7 0.0 copy-start.7
  8.7 0.0 copy-start.8
  8.7 0.0 copy-start.9
  8.8 0.0 copy-start.10
  8.8 8.0 %maximum_convert_fusion = f32[32,22,8192]{2,0,1:T(8,128)} fusion(bf16[32,7,8192]{2,0,1:T(8,128)(2,1)S(1)} %broadcast_in_dim.15, bf16[32,8,8192]{2,0,1:T(8,128)(2,1)S(1)} %bitcast.158), kind=kLoop, calls=%fused_computation.27 | loop fusion | flops 17301504 | bytes 30932992 | tf_op jit(solution)/shard_map/convert_element_type | solution.py:72
  16.8 0.0 copy-done.3
  16.8 0.0 copy-done.4
  16.8 0.0 copy-done.5
  16.8 0.0 copy-done.6
  16.8 0.0 copy-done.7
  16.8 50.0 %fusion.1 = f32[32,15,8192]{2,0,1:T(8,128)} fusion(f32[32,22,8192]{2,0,1:T(8,128)} %maximum_convert_fusion, f32[8192]{0:T(1024)S(1)} %copy-done.3, f32[8192]{0:T(1024)S(1)} %copy-done.4, f32[8192]{0:T(1024)S(1)} %copy-done.5, f32[8192]{0:T(1024)S(1)} %copy-done.6, f32[8192]{0:T(1024)S(1)} %copy-done.7, f32[8192]{0:T(1024)S(1)} %copy-done.8, ...), kind=kLoop, calls=%fused_computation.4 | loop fusion | flops 58982400 | bytes 141819904 | tf_op jit(solution)/shard_map/add | solution.py:75
  66.9 13.2 %fusion.19 = (f32[1,1,32,15,4096]{4,2,3,1,0:T(8,128)S(1)}, f32[1,32,15,4096]{3,1,2,0:T(8,128)}, f32[1,32,15,4096]{3,1,2,0:T(8,128)}, f32[1,1,32,15,4096]{4,2,3,1,0:T(8,128)}) fusion(f32[32,15,8192]{2,0,1:T(8,128)} %fusion.1), kind=kLoop, calls=%fused_computation.38 | loop fusion | flops 3932160 | bytes 47185920 | tf_op jit(solution)/shard_map/stack | solution.py:77
  80.1 5.3 %reduce-precision_convert_fusion = (bf16[2,1,32,15,4096]{4,2,3,1,0:T(8,128)(2,1)S(1)}, bf16[2,1,32,15,4096]{4,2,3,1,0:T(8,128)(2,1)S(1)}) fusion(f32[1,1,32,15,4096]{4,2,3,1,0:T(8,128)} %get-tuple-element.22, f32[1,1,32,15,4096]{4,2,3,1,0:T(8,128)S(1)} %get-tuple-element.19), kind=kLoop, calls=%fused_computation.1 | loop fusion | flops 19660800 | bytes 31457280 | tf_op jit(solution)/shard_map/convert_element_type | solution.py:32
  85.4 0.0 copy-start
  85.4 7.1 %fusion.8 = f32[2,2,32,15,256]{4,2,3,1,0:T(8,128)} fusion(bf16[2,1,32,15,4096]{4,2,3,1,0:T(8,128)(2,1)S(1)} %get-tuple-element.18, bf16[2,1,32,15,4096]{4,2,3,1,0:T(8,128)(2,1)S(1)} %get-tuple-element.17, bf16[2,4096,256]{2,1,0:T(8,128)(2,1)} %get-tuple-element.23), kind=kOutput, calls=%fused_computation.19 | convolution fusion | flops 4034396160 | bytes 21889024 | tf_op jit(solution)/shard_map/qhism,qmk->qhisk/dot_general | solution.py:81
  92.5 7.3 %fusion.22 = f32[2,32,15,256]{3,1,2,0:T(8,128)S(1)} fusion(bf16[2,4096,256]{2,1,0:T(8,128)(2,1)} %get-tuple-element.24, f32[1,32,15,4096]{3,1,2,0:T(8,128)S(1)} %copy-done, f32[1,32,15,4096]{3,1,2,0:T(8,128)} %get-tuple-element.21, f32[2,2,32,15,256]{4,2,3,1,0:T(8,128)} %fusion.8), kind=kOutput, calls=%fused_computation.41 | convolution fusion | flops 2025553920 | bytes 22872064 | tf_op jit(solution)/shard_map/qism,qmk->qisk/dot_general | solution.py:82
  99.8 4.2 %collective-permute-start = (f32[2,32,7,256]{3,1,2,0:T(8,128)S(1)}, f32[2,32,7,256]{3,1,2,0:T(8,128)S(1)}, u32[]{:S(2)}, u32[]{:S(2)}) collective-permute-start(f32[2,32,7,256]{3,1,2,0:T(8,128)S(1)} %slice.160), channel_id=1, source_target_pairs={{0,32},{32,64},{64,96},{96,128},{128,160},{160,192},{192,224},{1,3... | collective-permute-start | bytes 1376264 | tf_op jit(solution)/shard_map/ppermute | solution.py:15
  104.1 0.1 copy.814
  104.2 0.1 copy.818
  104.3 0.1 copy.815
  104.4 8.6 %collective-permute-done = f32[2,32,7,256]{3,1,2,0:T(8,128)S(1)} collective-permute-done((f32[2,32,7,256]{3,1,2,0:T(8,128)S(1)}, f32[2,32,7,256]{3,1,2,0:T(8,128)S(1)}, u32[]{:S(2)}, u32[]{:S(2)}) %collective-permute-start) | collective-permute-done | bytes 458784 | tf_op jit(solution)/shard_map/ppermute | solution.py:15
  113.0 0.1 fusion.33
  113.0 0.3 reshape.268
  113.3 0.6 fusion.61
  113.9 0.3 fusion.45
  114.3 6.7 %copy.820 = bf16[128,2,32,2,8]{4,3,2,1,0:T(2,128)(2,1)} copy(bf16[128,2,32,2,8]{0,4,3,2,1:T(8,128)(2,1)S(1)} %pad_maximum_fusion.1) | data formatting | bytes 524288 | tf_op jit(solution)/shard_map/stack | solution.py:94
  121.0 7.0 %convert_element_type.68 = bf16[8,32,512]{2,1,0:T(8,128)(2,1)S(1)} reshape(bf16[128,2,32,2,8]{4,3,2,1,0:T(2,128)(2,1)} %copy.820) | data formatting | bytes 524288 | tf_op jit(solution)/shard_map/convert_element_type | solution.py:94
  128.0 11.9 %all_to_all.10 = bf16[8,32,512]{2,1,0:T(8,128)(2,1)S(1)} all-to-all(bf16[8,32,512]{2,1,0:T(8,128)(2,1)S(1)} %convert_element_type.68), channel_id=1, replica_groups=mesh['tm'=8,'stn'=32] {'tm'}, dimensions={0} | all-to-all | bytes 524288 | tf_op jit(solution)/shard_map/all_to_all | solution.py:97
  140.0 0.2 fusion.63
  140.4 0.3 fusion.62
  141.0 26.8 %all_to_all.11 = bf16[32,8,1,512]{3,1,2,0:T(8,128)(2,1)S(1)} all-to-all(bf16[32,8,1,512]{3,1,2,0:T(8,128)(2,1)S(1)} %constant_dynamic-update-slice_fusion), channel_id=1, replica_groups=mesh['tm'=8,'stn'=32] {'stn'}, dimensions={0} | all-to-all | bytes 524288 | tf_op jit(solution)/shard_map/all_to_all | solution.py:99
  167.8 0.5 copy.821
  168.3 0.9 copy.822
  169.2 1.1 reshape_reshape.7
  170.3 1.1 reshape.270
  171.4 4.7 %convolution_multiply_fusion = f32[2048,1024]{1,0:T(8,128)} fusion(bf16[1024,128]{0,1:T(8,128)(2,1)S(1)} %reshape_reshape.7, bf16[1024,64]{0,1:T(8,128)(2,1)S(1)} %get-tuple-element.30, bf16[1024,64]{0,1:T(8,128)(2,1)S(1)} %get-tuple-element.29), kind=kOutput, calls=%fused_computation.33 | convolution fusion | flops 540540928 | bytes 8912896 | tf_op jit(solution)/shard_map/ik,jk->ij/dot_general | solution.py:107
  (46 shorter events, 0.4 us)
Async XLA Ops:
  2.6 5.4 %copy-start.1 = (bf16[32,65536]{1,0:T(8,128)(2,1)S(1)}, bf16[32,65536]{1,0:T(8,128)(2,1)}, u32[]{:S(2)}) copy-start(bf16[32,65536]{1,0:T(8,128)(2,1)} %param.5) | copy-start | bytes 12582916
  8.7 8.1 %copy-start.3 = (f32[8192]{0:T(1024)S(1)}, f32[8192]{0:T(1024)}, u32[]{:S(2)}) copy-start(f32[8192]{0:T(1024)} %constant.101) | copy-start | bytes 98308
  8.7 8.1 %copy-start.4 = (f32[8192]{0:T(1024)S(1)}, f32[8192]{0:T(1024)}, u32[]{:S(2)}) copy-start(f32[8192]{0:T(1024)} %constant.99) | copy-start | bytes 98308
  8.7 8.1 %copy-start.5 = (f32[8192]{0:T(1024)S(1)}, f32[8192]{0:T(1024)}, u32[]{:S(2)}) copy-start(f32[8192]{0:T(1024)} %constant.97) | copy-start | bytes 98308
  8.7 8.1 %copy-start.6 = (f32[8192]{0:T(1024)S(1)}, f32[8192]{0:T(1024)}, u32[]{:S(2)}) copy-start(f32[8192]{0:T(1024)} %constant.95) | copy-start | bytes 98308
  8.7 8.1 %copy-start.7 = (f32[8192]{0:T(1024)S(1)}, f32[8192]{0:T(1024)}, u32[]{:S(2)}) copy-start(f32[8192]{0:T(1024)} %constant.93) | copy-start | bytes 98308
  8.7 8.1 %copy-start.8 = (f32[8192]{0:T(1024)S(1)}, f32[8192]{0:T(1024)}, u32[]{:S(2)}) copy-start(f32[8192]{0:T(1024)} %constant.91) | copy-start | bytes 98308
  8.7 8.1 %copy-start.9 = (f32[8192]{0:T(1024)S(1)}, f32[8192]{0:T(1024)}, u32[]{:S(2)}) copy-start(f32[8192]{0:T(1024)} %constant.89) | copy-start | bytes 98308
  8.8 8.1 %copy-start.10 = (f32[8192]{0:T(1024)S(1)}, f32[8192]{0:T(1024)}, u32[]{:S(2)}) copy-start(f32[8192]{0:T(1024)} %constant.87) | copy-start | bytes 98308
  85.4 7.1 %copy-start = (f32[1,32,15,4096]{3,1,2,0:T(8,128)S(1)}, f32[1,32,15,4096]{3,1,2,0:T(8,128)}, u32[]{:S(2)}) copy-start(f32[1,32,15,4096]{3,1,2,0:T(8,128)} %get-tuple-element.20) | copy-start | bytes 23592964
  92.5 11.6 %copy-start.2 = (f32[2,32,256]{2,1,0:T(8,128)S(1)}, f32[2,32,256]{2,1,0:T(8,128)}, u32[]{:S(2)}) copy-start(f32[2,32,256]{2,1,0:T(8,128)} %param.6) | copy-start | bytes 196612
  99.8 13.1 %collective-permute-start = (f32[2,32,7,256]{3,1,2,0:T(8,128)S(1)}, f32[2,32,7,256]{3,1,2,0:T(8,128)S(1)}, u32[]{:S(2)}, u32[]{:S(2)}) collective-permute-start(f32[2,32,7,256]{3,1,2,0:T(8,128)S(1)} %slice.160), channel_id=1, source_target_pairs={{0,32},{32,64},{64,96},{96,128},{128,160},{160,192},{192,224},{1,3... | collective-permute-start | bytes 1376264 | tf_op jit(solution)/shard_map/ppermute | solution.py:15
